TPU v7x, 32 devices: a whole 2x2x4 slice. The times are simulated.
32 devices in a mesh: shard: 2 (over core), context: 4 (over z), tensor: 4 (over y, x).
Axes of the slice: x: 2, y: 2, z: 4, core: 2. Of those that a mesh axis runs over, the one named last changes fastest.
Arguments:
- inputs: bfloat16 [2, 2048, 2048], P('shard', 'context'), may hold values from -6 to 6
- segments: int32 [2, 2048], P('shard', 'context'), may hold values from 0 to 2, as said below
- positions: int32 [2, 2048], P('shard', 'context'), may hold values from 0 to 2047, as said below
- w_q: bfloat16 [2048, 2048], P(('shard', 'context'), 'tensor'), may hold values from -0.125 to 0.125
- w_k: bfloat16 [2048, 2048], P(('shard', 'context'), 'tensor'), may hold values from -0.125 to 0.125
- w_v: bfloat16 [2048, 2048], P(('shard', 'context'), 'tensor'), may hold values from -0.125 to 0.125
- w_o: bfloat16 [2048, 2048], P(('shard', 'context'), 'tensor'), may hold values from -0.75 to 0.75
- w_gate: bfloat16 [2048, 8192], P(('shard', 'context'), 'tensor'), may hold values from -0.125 to 0.125
- w_up: bfloat16 [2048, 8192], P(('shard', 'context'), 'tensor'), may hold values from -0.125 to 0.125
- w_down: bfloat16 [2048, 8192], P(('shard', 'context'), 'tensor'), may hold values from -0.0625 to 0.0625
- g_attn: bfloat16 [2048], P(('shard', 'context')), may hold values from 0.5 to 1.5
- g_mlp: bfloat16 [2048], P(('shard', 'context')), may hold values from 0.5 to 1.5
- d_out: bfloat16 [2, 2048, 2048], P('shard', 'context'), may hold values from -6 to 6
Outputs:
- out: bfloat16 [2, 2048, 2048], P('shard', 'context')
- d_x: bfloat16 [2, 2048, 2048], P('shard', 'context')
- d_w_q: float32 [2048, 2048], P(('shard', 'context'), 'tensor')
- d_w_k: float32 [2048, 2048], P(('shard', 'context'), 'tensor')
- d_w_v: float32 [2048, 2048], P(('shard', 'context'), 'tensor')
- d_w_o: float32 [2048, 2048], P(('shard', 'context'), 'tensor')
- d_w_gate: float32 [2048, 8192], P(('shard', 'context'), 'tensor')
- d_w_up: float32 [2048, 8192], P(('shard', 'context'), 'tensor')
- d_w_down: float32 [2048, 8192], P(('shard', 'context'), 'tensor')
- d_g_attn: float32 [2048], P(('shard', 'context'))
- d_g_mlp: float32 [2048], P(('shard', 'context'))
Inputs may be any that keep to these rules, and one draw needn't show every extreme that they name: In each sequence the positions are a permutation of 0 to 2047, laid out by halves of 512 tokens: with p a permutation of the context indices, device c holds either halves 2 * p(c) and 2 * p(c) + 1 in order, or halves p(c) and 7 - p(c). `segments`: segment numbers never fall as the position grows; the first position of a sequence is in segment 0, and every sequence holds exactly 3 documents.
All inputs are finite; a program needn't handle non-finite values.
Results may differ from a plain program's by a relative error of at most 0.024.
Values may be sent and summed in bfloat16 or wider, within the bound.
No kernel may reach another device: no remote copies, remote signals or barrier semaphores. Data moves between devices by JAX's collectives and lax.ppermute only.
A program may use at most 192 MiB of HBM per device.

v0:
```python
import math
import jax
import jax.numpy as jnp
from jax import lax
from jax.sharding import PartitionSpec as P

HD = 64
EPS = 1e-05
THETA = 130000.0
NEG = -1e30


def passed_along(value, axis, steps):
    count = lax.axis_size(axis)
    pairs = [(source, (source + steps) % count) for source in range(count)]
    return lax.ppermute(value, axis, pairs)


def rope_tables(position):
    index = jnp.arange(HD // 2, dtype=jnp.float32)
    inverse = jnp.power(jnp.float32(THETA), -2.0 * index / HD)
    angle = position.astype(jnp.float32)[:, None] * inverse[None, :]
    return (jnp.cos(angle), jnp.sin(angle))


def rotate(tensor, cosine, sine):
    half = tensor.shape[-1] // 2
    first = tensor[..., :half]
    second = tensor[..., half:]
    cosine = cosine[:, None, :]
    sine = sine[:, None, :]
    return jnp.concatenate(
        [first * cosine - second * sine, second * cosine + first * sine], axis=-1
    )


def rotate_back(grad, cosine, sine):
    half = grad.shape[-1] // 2
    first = grad[..., :half]
    second = grad[..., half:]
    cosine = cosine[:, None, :]
    sine = sine[:, None, :]
    return jnp.concatenate(
        [first * cosine + second * sine, second * cosine - first * sine], axis=-1
    )


def normalize(value):
    inv_rms = lax.rsqrt(jnp.mean(value * value, axis=-1, keepdims=True) + EPS)
    return (value * inv_rms, inv_rms)


def norm_back(grad, normed, inv_rms, gain):
    scaled = grad * gain.astype(jnp.float32)
    return inv_rms * (scaled - normed * jnp.mean(scaled * normed, axis=-1, keepdims=True))


def contract_last(left, right):
    return lax.dot_general(
        left, right, (((1,), (1,)), ((), ())), preferred_element_type=jnp.float32
    )


def contract_first(left, right):
    return lax.dot_general(
        left, right, (((0,), (0,)), ((), ())), preferred_element_type=jnp.float32
    )


def branch_total(partial_sum):
    return lax.psum(partial_sum.astype(jnp.bfloat16), "tensor").astype(jnp.float32)


def input_total(partial_sum):
    return lax.psum(partial_sum.astype(jnp.bfloat16), "tensor").astype(jnp.float32)


def pass_grads(grad_key, grad_value):
    return (
        passed_along(grad_key.astype(jnp.bfloat16), "context", 1).astype(grad_key.dtype),
        passed_along(grad_value.astype(jnp.bfloat16), "context", 1).astype(grad_value.dtype),
    )


def key_scores(query_heads, query_seg, query_pos, piece):
    key_flat, value_flat, key_seg, key_pos = piece
    heads = query_heads.shape[1]
    key_heads = key_flat.reshape(key_flat.shape[0], heads, HD)
    value_heads = value_flat.reshape(value_flat.shape[0], heads, HD)
    scores = jnp.einsum(
        "qhd,khd->hqk", query_heads, key_heads, preferred_element_type=jnp.float32
    ) * (1.0 / math.sqrt(HD))
    allowed = (query_seg[:, None] == key_seg[None, :]) & (key_pos[None, :] <= query_pos[:, None])
    return (jnp.where(allowed[None], scores, NEG), allowed, key_heads, value_heads)


def forward_fold(stats, piece, query_heads, query_seg, query_pos):
    peak, total, accum = stats
    scores, allowed, key_heads, value_heads = key_scores(query_heads, query_seg, query_pos, piece)
    new_peak = jnp.maximum(peak, jnp.max(scores, axis=-1))
    weights = jnp.where(allowed[None], jnp.exp(scores - new_peak[..., None]), 0.0)
    factor = jnp.exp(peak - new_peak)
    total = total * factor + jnp.sum(weights, axis=-1)
    accum = accum * factor[..., None] + jnp.einsum(
        "hqk,khd->hqd",
        weights.astype(jnp.bfloat16),
        value_heads,
        preferred_element_type=jnp.float32,
    )
    return (new_peak, total, accum)


def backward_piece(piece, query_heads, grad_heads, log_total, inner, query_seg, query_pos):
    scores, allowed, key_heads, value_heads = key_scores(query_heads, query_seg, query_pos, piece)
    probs = jnp.where(allowed[None], jnp.exp(scores - log_total[..., None]), 0.0)
    grad_value = jnp.einsum(
        "hqk,qhd->khd", probs.astype(jnp.bfloat16), grad_heads, preferred_element_type=jnp.float32
    )
    grad_probs = jnp.einsum(
        "qhd,khd->hqk", grad_heads, value_heads, preferred_element_type=jnp.float32
    )
    grad_scores = (probs * (grad_probs - inner[..., None]) * (1.0 / math.sqrt(HD))).astype(
        jnp.bfloat16
    )
    grad_query = jnp.einsum(
        "hqk,khd->qhd", grad_scores, key_heads, preferred_element_type=jnp.float32
    )
    grad_key = jnp.einsum(
        "hqk,qhd->khd", grad_scores, query_heads, preferred_element_type=jnp.float32
    )
    key_rows = grad_key.shape[0]
    return (grad_query, grad_key.reshape(key_rows, -1), grad_value.reshape(key_rows, -1))


def on_device(
    inputs, segments, positions, w_q, w_k, w_v, w_o, w_gate, w_up, w_down, g_attn, g_mlp, d_out
):
    f32 = jnp.float32
    bf16 = jnp.bfloat16
    rows = inputs.shape[1]
    width = inputs.shape[2]
    tokens = inputs.reshape(rows, width)
    segment = segments.reshape(rows)
    position = positions.reshape(rows)
    fetched = (
        lax.all_gather(w_q, ("shard", "context"), axis=0, tiled=True),
        lax.all_gather(w_k, ("shard", "context"), axis=0, tiled=True),
        lax.all_gather(w_v, ("shard", "context"), axis=0, tiled=True),
        lax.all_gather(w_o, ("shard", "context"), axis=0, tiled=True),
        lax.all_gather(w_gate, ("shard", "context"), axis=0, tiled=True),
        lax.all_gather(w_up, ("shard", "context"), axis=0, tiled=True),
        lax.all_gather(w_down, ("shard", "context"), axis=0, tiled=True),
        lax.all_gather(g_attn, ("shard", "context"), axis=0, tiled=True),
        lax.all_gather(g_mlp, ("shard", "context"), axis=0, tiled=True),
    )
    full_q, full_k, full_v, full_o, full_gate, full_up, full_down, gain_attn, gain_mlp = fetched
    heads = full_q.shape[1] // HD
    cosine, sine = rope_tables(position)
    resid1 = tokens.astype(f32)
    norm1, inv1 = normalize(resid1)
    h1 = (norm1 * gain_attn.astype(f32)).astype(bf16)
    query = rotate(
        jnp.dot(h1, full_q, preferred_element_type=f32).reshape(rows, heads, HD), cosine, sine
    ).astype(bf16)
    key_flat = (
        rotate(
            jnp.dot(h1, full_k, preferred_element_type=f32).reshape(rows, heads, HD), cosine, sine
        )
        .astype(bf16)
        .reshape(rows, heads * HD)
    )
    value_flat = jnp.dot(h1, full_v, preferred_element_type=f32).astype(bf16)
    start_stats = (
        jnp.full((heads, rows), NEG, f32),
        jnp.zeros((heads, rows), f32),
        jnp.zeros((heads, rows, HD), f32),
    )
    stats = forward_fold(
        start_stats, (key_flat, value_flat, segment, position), query, segment, position
    )

    def cycle_turn(index, carry):
        moving_key, moving_value, moving_seg, moving_pos, current = carry
        moving_key, moving_value, moving_seg, moving_pos = passed_along(
            (moving_key, moving_value, moving_seg, moving_pos), "context", 1
        )
        current = forward_fold(
            current, (moving_key, moving_value, moving_seg, moving_pos), query, segment, position
        )
        return (moving_key, moving_value, moving_seg, moving_pos, current)

    stats = lax.fori_loop(
        0,
        lax.axis_size("context") - 1,
        cycle_turn,
        (key_flat, value_flat, segment, position, stats),
    )[4]
    peak, total, accum = stats
    attended = jnp.transpose(accum / total[..., None], (1, 0, 2)).astype(bf16)
    log_total = peak + jnp.log(total)
    attended_flat = attended.reshape(rows, heads * HD)
    attn_partial = contract_last(attended_flat, full_o)
    resid2 = resid1 + branch_total(attn_partial)
    norm2, inv2 = normalize(resid2)
    h2_part = (norm2 * gain_mlp.astype(f32)).astype(bf16)
    gate = jnp.dot(h2_part, full_gate, preferred_element_type=f32)
    up = jnp.dot(h2_part, full_up, preferred_element_type=f32)
    active = jax.nn.silu(gate)
    hidden = (active * up).astype(bf16)
    mlp_partial = contract_last(hidden, full_down)
    result = (resid2 + branch_total(mlp_partial)).astype(bf16)
    fetched = (
        lax.all_gather(w_q, ("shard", "context"), axis=0, tiled=True),
        lax.all_gather(w_k, ("shard", "context"), axis=0, tiled=True),
        lax.all_gather(w_v, ("shard", "context"), axis=0, tiled=True),
        lax.all_gather(w_o, ("shard", "context"), axis=0, tiled=True),
        lax.all_gather(w_gate, ("shard", "context"), axis=0, tiled=True),
        lax.all_gather(w_up, ("shard", "context"), axis=0, tiled=True),
        lax.all_gather(w_down, ("shard", "context"), axis=0, tiled=True),
        lax.all_gather(g_attn, ("shard", "context"), axis=0, tiled=True),
        lax.all_gather(g_mlp, ("shard", "context"), axis=0, tiled=True),
    )
    full_q, full_k, full_v, full_o, full_gate, full_up, full_down, gain_attn, gain_mlp = fetched
    grad_y = d_out.reshape(rows, width)
    grad_hidden = jnp.dot(grad_y, full_down, preferred_element_type=f32)
    sigma = jax.nn.sigmoid(gate)
    grad_gate = (grad_hidden * up * sigma * (1.0 + gate * (1.0 - sigma))).astype(bf16)
    grad_up = (grad_hidden * active).astype(bf16)
    h2_grad_partial = contract_last(grad_gate, full_gate) + contract_last(grad_up, full_up)
    grad_h2 = input_total(h2_grad_partial)
    grad_gmlp = jnp.sum(grad_h2 * norm2, axis=0)
    grad_resid = grad_y.astype(f32) + norm_back(grad_h2, norm2, inv2, gain_mlp)
    grad_resid_part = grad_resid.astype(bf16)
    grad_heads = (
        jnp.dot(grad_resid_part, full_o, preferred_element_type=f32)
        .astype(bf16)
        .reshape(rows, heads, HD)
    )
    inner = jnp.sum(grad_heads.astype(f32) * attended.astype(f32), axis=-1).T

    def piece_grads(piece):
        return backward_piece(piece, query, grad_heads, log_total, inner, segment, position)

    grad_query, grad_key, grad_value = piece_grads((key_flat, value_flat, segment, position))

    def grad_turn(index, carry):
        moving_key, moving_value, moving_seg, moving_pos, acc_query, acc_key, acc_value = carry
        moving_key, moving_value, moving_seg, moving_pos = passed_along(
            (moving_key, moving_value, moving_seg, moving_pos), "context", 1
        )
        acc_key, acc_value = pass_grads(acc_key, acc_value)
        part_query, part_key, part_value = piece_grads(
            (moving_key, moving_value, moving_seg, moving_pos)
        )
        return (
            moving_key,
            moving_value,
            moving_seg,
            moving_pos,
            acc_query + part_query,
            acc_key + part_key,
            acc_value + part_value,
        )

    carried = lax.fori_loop(
        0,
        lax.axis_size("context") - 1,
        grad_turn,
        (key_flat, value_flat, segment, position, grad_query, grad_key, grad_value),
    )
    grad_query = carried[4]
    grad_key, grad_value = pass_grads(carried[5], carried[6])
    grad_qin = rotate_back(grad_query, cosine, sine).astype(bf16).reshape(rows, heads * HD)
    grad_kin = (
        rotate_back(grad_key.reshape(rows, heads, HD), cosine, sine)
        .astype(bf16)
        .reshape(rows, heads * HD)
    )
    grad_vin = grad_value.astype(bf16)
    h1_grad_partial = (
        contract_last(grad_qin, full_q)
        + contract_last(grad_kin, full_k)
        + contract_last(grad_vin, full_v)
    )
    grad_h1 = input_total(h1_grad_partial)
    grad_gattn = jnp.sum(grad_h1 * norm1, axis=0)
    grad_x_part = (grad_resid + norm_back(grad_h1, norm1, inv1, gain_attn)).astype(bf16)
    grad_wq = contract_first(h1, grad_qin)
    grad_wk = contract_first(h1, grad_kin)
    grad_wv = contract_first(h1, grad_vin)
    grad_wo = contract_first(grad_resid_part, attended_flat)
    grad_wgate = contract_first(h2_part, grad_gate)
    grad_wup = contract_first(h2_part, grad_up)
    grad_wdown = contract_first(grad_y, hidden)
    reduced = (
        lax.psum_scatter(
            grad_wq.astype(jnp.bfloat16), ("shard", "context"), scatter_dimension=0, tiled=True
        ).astype(jnp.float32),
        lax.psum_scatter(
            grad_wk.astype(jnp.bfloat16), ("shard", "context"), scatter_dimension=0, tiled=True
        ).astype(jnp.float32),
        lax.psum_scatter(
            grad_wv.astype(jnp.bfloat16), ("shard", "context"), scatter_dimension=0, tiled=True
        ).astype(jnp.float32),
        lax.psum_scatter(
            grad_wo.astype(jnp.bfloat16), ("shard", "context"), scatter_dimension=0, tiled=True
        ).astype(jnp.float32),
        lax.psum_scatter(
            grad_wgate.astype(jnp.bfloat16), ("shard", "context"), scatter_dimension=0, tiled=True
        ).astype(jnp.float32),
        lax.psum_scatter(
            grad_wup.astype(jnp.bfloat16), ("shard", "context"), scatter_dimension=0, tiled=True
        ).astype(jnp.float32),
        lax.psum_scatter(
            grad_wdown.astype(jnp.bfloat16), ("shard", "context"), scatter_dimension=0, tiled=True
        ).astype(jnp.float32),
        lax.psum_scatter(
            grad_gattn.astype(jnp.bfloat16), ("shard", "context"), scatter_dimension=0, tiled=True
        ).astype(jnp.float32),
        lax.psum_scatter(
            grad_gmlp.astype(jnp.bfloat16), ("shard", "context"), scatter_dimension=0, tiled=True
        ).astype(jnp.float32),
    )
    return (
        result.reshape(1, rows, width),
        grad_x_part.reshape(1, rows, width),
        reduced[0],
        reduced[1],
        reduced[2],
        reduced[3],
        reduced[4],
        reduced[5],
        reduced[6],
        reduced[7],
        reduced[8],
    )


def solution(mesh):
    placed = (
        P("shard", "context", None),
        P("shard", "context"),
        P("shard", "context"),
        P(("shard", "context"), "tensor"),
        P(("shard", "context"), "tensor"),
        P(("shard", "context"), "tensor"),
        P(("shard", "context"), "tensor"),
        P(("shard", "context"), "tensor"),
        P(("shard", "context"), "tensor"),
        P(("shard", "context"), "tensor"),
        P(("shard", "context")),
        P(("shard", "context")),
        P("shard", "context", None),
    )
    return jax.shard_map(
        on_device,
        mesh=mesh,
        in_specs=placed,
        out_specs=(
            P("shard", "context", None),
            P("shard", "context", None),
            P(("shard", "context"), "tensor"),
            P(("shard", "context"), "tensor"),
            P(("shard", "context"), "tensor"),
            P(("shard", "context"), "tensor"),
            P(("shard", "context"), "tensor"),
            P(("shard", "context"), "tensor"),
            P(("shard", "context"), "tensor"),
            P(("shard", "context")),
            P(("shard", "context")),
        ),
        check_vma=False,
    )
```

profile of v0, /device:TPU:0, one launch (start us, length us, event | category | flops | bytes accessed | tf_op | source)
XLA Modules:
  0.0 1685.4 jit_solution(14790218301723463259)
XLA Ops:
  16.6 18.3 %all-gather = bf16[8,1,256]{2,1,0:T(2,128)(2,1)S(1)} all-gather(bf16[1,1,256]{2,1,0:T(2,128)(2,1)S(1)} %reshape.451), channel_id=1, replica_groups=mesh['shard'=2,'context'=4,'tensor'=4] {'shard','context'}, dimensions={0}, use_global_device_ids=true | all-gather | bytes 4608 | tf_op jit(solution)/shard_map/all_gather | solution.py:153
  46.8 25.0 %all-gather.10.cloned.1.call-done = bf16[2048,512]{1,0:T(8,128)(2,1)} async-done(((bf16[256,512]{1,0:T(8,128)(2,1)}), bf16[2048,512]{1,0:T(8,128)(2,1)}) %all-gather.10.cloned.1.call-update) | async-done | bytes 2097168 | tf_op jit(solution)/shard_map/all_gather | solution.py:147
  80.5 21.5 %all-gather.14.cloned.1.call-done = bf16[2048,512]{1,0:T(8,128)(2,1)} async-done(((bf16[256,512]{1,0:T(8,128)(2,1)}), bf16[2048,512]{1,0:T(8,128)(2,1)}) %all-gather.14.cloned.1.call-update) | async-done | bytes 2097168 | tf_op jit(solution)/shard_map/all_gather | solution.py:146
  117.3 105.5 %while.44 = (s32[]{:T(128)}, bf16[512,512]{0,1:T(8,128)(2,1)}, bf16[512,512]{0,1:T(8,128)(2,1)}, s32[512]{0:T(512)S(1)}, s32[512]{0:T(512)S(1)}, /*index=5*/f32[...) while((s32[]{:T(128)}, bf16[512,512]{0,1:T(8,128)(2,1)}, ...), condition=%wide.region_6.7_spmd, body=%wide.region_3.6_spmd.sunk | while | flops 565452800 | bytes 44859724 | solution.py:192
  122.5 20.8 %collective-permute-done.3 = s32[512]{0:T(512)S(1)} collective-permute-done((s32[512]{0:T(512)S(1)}, s32[512]{0:T(512)S(1)}, u32[]{:S(2)}, u32[]{:S(2)}) %collective-permute-start.3) | collective-permute-done | bytes 2080 | tf_op jit(solution)/shard_map/while/body/eval_jaxpr/ppermute | solution.py:16
  164.3 12.0 collective-permute-done.3
  196.5 12.0 collective-permute-done.3
  230.8 12.8 all-gather.1
  243.6 52.8 %all-reduce.8.cloned.1.call-done = bf16[512,2048]{1,0:T(8,128)(2,1)} async-done(((bf16[512,2048]{1,0:T(8,128)(2,1)}), bf16[512,2048]{1,0:T(8,128)(2,1)}) %all-reduce.8.cloned.1.call-update) | async-done | bytes 2097168 | tf_op jit(solution)/shard_map/psum | solution.py:71
  301.3 78.6 %all-gather.20.cloned.1.call-done = bf16[2048,2048]{1,0:T(8,128)(2,1)} async-done(((bf16[256,2048]{1,0:T(8,128)(2,1)}), bf16[2048,2048]{1,0:T(8,128)(2,1)}) %all-gather.20.cloned.1.call-update) | async-done | bytes 8388624 | tf_op jit(solution)/shard_map/all_gather | solution.py:151
  379.9 10.6 fusion.91
  390.5 71.6 %all-gather.18.cloned.1.call-done = bf16[2048,2048]{1,0:T(8,128)(2,1)} async-done(((bf16[256,2048]{1,0:T(8,128)(2,1)}), bf16[2048,2048]{1,0:T(8,128)(2,1)}) %all-gather.18.cloned.1.call-update) | async-done | bytes 8388624 | tf_op jit(solution)/shard_map/all_gather | solution.py:150
  462.1 10.6 fusion.90
  472.7 71.6 %all-gather.22.cloned.1.call-done = bf16[2048,2048]{1,0:T(8,128)(2,1)} async-done(((bf16[256,2048]{1,0:T(8,128)(2,1)}), bf16[2048,2048]{1,0:T(8,128)(2,1)}) %all-gather.22.cloned.1.call-update) | async-done | bytes 8388624 | tf_op jit(solution)/shard_map/all_gather | solution.py:152
  544.3 14.1 multiply_convert_fusion.2
  572.4 67.9 %all-reduce.10.cloned.1.call-done = bf16[512,2048]{1,0:T(8,128)(2,1)} async-done(((bf16[512,2048]{1,0:T(8,128)(2,1)}), bf16[512,2048]{1,0:T(8,128)(2,1)}) %all-reduce.10.cloned.1.call-update) | async-done | bytes 2097168 | tf_op jit(solution)/shard_map/psum | solution.py:75
  665.3 227.0 %while.45 = (s32[]{:T(128)}, bf16[512,512]{0,1:T(8,128)(2,1)}, bf16[512,512]{0,1:T(8,128)(2,1)}, s32[512]{0:T(512)S(1)}, s32[512]{0:T(512)S(1)}, /*index=5*/f32[...) while((s32[]{:T(128)}, bf16[512,512]{0,1:T(8,128)(2,1)}, ...), condition=%wide.region_14.15_spmd, body=%wide.region_13.14_spmd.sunk | while | flops 1372061696 | bytes 71647696 | solution.py:265
  671.8 17.6 %collective-permute-done.7 = s32[512]{0:T(512)S(1)} collective-permute-done((s32[512]{0:T(512)S(1)}, s32[512]{0:T(512)S(1)}, u32[]{:S(2)}, u32[]{:S(2)}) %collective-permute-start.7) | collective-permute-done | bytes 2080 | tf_op jit(solution)/shard_map/while/body/eval_jaxpr/ppermute | solution.py:16
  692.6 61.4 %collective-permute-done.5 = bf16[512,512]{0,1:T(8,128)(2,1)S(1)} collective-permute-done((bf16[512,512]{0,1:T(8,128)(2,1)}, bf16[512,512]{0,1:T(8,128)(2,1)S(1)}, u32[]{:S(2)}, u32[]{:S(2)}) %collective-permute-start.5) | collective-permute-done | bytes 524320 | tf_op jit(solution)/shard_map/while/body/eval_jaxpr/ppermute | solution.py:16
  773.6 11.9 collective-permute-done.7
  787.2 29.1 %collective-permute-done.5 = bf16[512,512]{0,1:T(8,128)(2,1)S(1)} collective-permute-done((bf16[512,512]{0,1:T(8,128)(2,1)}, bf16[512,512]{0,1:T(8,128)(2,1)S(1)}, u32[]{:S(2)}, u32[]{:S(2)}) %collective-permute-start.5) | collective-permute-done | bytes 524320 | tf_op jit(solution)/shard_map/while/body/eval_jaxpr/ppermute | solution.py:16
  835.9 11.9 collective-permute-done.7
  849.4 28.2 %collective-permute-done.5 = bf16[512,512]{0,1:T(8,128)(2,1)S(1)} collective-permute-done((bf16[512,512]{0,1:T(8,128)(2,1)}, bf16[512,512]{0,1:T(8,128)(2,1)S(1)}, u32[]{:S(2)}, u32[]{:S(2)}) %collective-permute-start.5) | collective-permute-done | bytes 524320 | tf_op jit(solution)/shard_map/while/body/eval_jaxpr/ppermute | solution.py:16
  892.4 12.1 collective-permute-done.11
  908.1 19.6 %collective-permute-done.10 = bf16[512,512]{0,1:T(8,128)(2,1)S(1)} collective-permute-done((bf16[512,512]{0,1:T(8,128)(2,1)}, bf16[512,512]{0,1:T(8,128)(2,1)S(1)}, u32[]{:S(2)}, u32[]{:S(2)}) %collective-permute-start.10) | collective-permute-done | bytes 524320 | tf_op jit(solution)/shard_map/ppermute | solution.py:16
  987.0 21.2 %reduce-scatter.10.cloned.1.call-done = bf16[256,512]{1,0:T(8,128)(2,1)} async-done(((bf16[2048,512]{1,0:T(8,128)(2,1)}), bf16[256,512]{1,0:T(8,128)(2,1)}) %reduce-scatter.10.cloned.1.call-update) | async-done | bytes 262160 | tf_op jit(solution)/shard_map/reduce_scatter | solution.py:299
  1009.9 49.3 %reduce-scatter.8.cloned.1.call-done = bf16[256,512]{1,0:T(8,128)(2,1)} async-done(((bf16[2048,512]{1,0:T(8,128)(2,1)}), bf16[256,512]{1,0:T(8,128)(2,1)}) %reduce-scatter.8.cloned.1.call-update) | async-done | bytes 262160 | tf_op jit(solution)/shard_map/reduce_scatter | solution.py:296
  1061.1 105.0 %all-reduce.12.cloned.1.call-done = (bf16[512,2048]{1,0:T(8,128)(2,1)}, bf16[512,2048]{1,0:T(8,128)(2,1)}) async-done(((bf16[512,2048]{1,0:T(8,128)(2,1)}, bf16[512,2048]{1,0:T(8,128)(2,1)}), (bf16[512,2048]{1,0:T(8,128)(2,1)}, bf16[512,2048]{1,0:T(8,128)(2,1)})) %all-reduce.12.cloned.1.call-update) | async-done | bytes 4194320 | tf_op jit(solution)/shard_map/psum | solution.py:71
  1168.9 19.6 %all-reduce.2 = (bf16[2048]{0:T(1024)(128)(2,1)S(1)}, bf16[2048]{0:T(1024)(128)(2,1)S(1)}) all-reduce(bf16[2048]{0:T(1024)(128)(2,1)S(1)} %get-tuple-element.174, bf16[2048]{0:T(1024)(128)(2,1)S(1)} %copy-done.44), channel_id=9, replica_groups=mesh['shard'=2,'context'=4,'tensor'=4] {'shard','context'}, use_global_device_ids=true, to_apply=%region_25.26.clone | all-reduce | flops 4096 | bytes 16384
  1197.9 137.8 %reduce-scatter.20.cloned.1.call-done = bf16[256,2048]{0,1:T(8,128)(2,1)} async-done(((bf16[2048,2048]{0,1:T(8,128)(2,1)}), bf16[256,2048]{0,1:T(8,128)(2,1)}) %reduce-scatter.20.cloned.1.call-update) | async-done | bytes 1048592 | tf_op jit(solution)/shard_map/reduce_scatter | solution.py:314
  1338.3 167.5 %reduce-scatter.18.cloned.1.call-done = bf16[256,2048]{1,0:T(8,128)(2,1)} async-done(((bf16[2048,2048]{1,0:T(8,128)(2,1)}), bf16[256,2048]{1,0:T(8,128)(2,1)}) %reduce-scatter.18.cloned.1.call-update) | async-done | bytes 1048592 | tf_op jit(solution)/shard_map/reduce_scatter | solution.py:311
  1508.6 167.3 %reduce-scatter.16.cloned.1.call-done = bf16[256,2048]{1,0:T(8,128)(2,1)} async-done(((bf16[2048,2048]{1,0:T(8,128)(2,1)}), bf16[256,2048]{1,0:T(8,128)(2,1)}) %reduce-scatter.16.cloned.1.call-update) | async-done | bytes 1048592 | tf_op jit(solution)/shard_map/reduce_scatter | solution.py:308
  (365 shorter events, 309.8 us)
Async XLA Ops:
  7.2 34.5 %all-gather.12.cloned.1.call-start = ((), (), s32[]{:S(2)}) async-start(), calls=%async_computation.8 | async-start | bytes 2359296 | tf_op jit(solution)/shard_map/all_gather | solution.py:148
  7.9 63.9 %all-gather.10.cloned.1.call-start = ((), (), s32[]{:S(2)}) async-start(), calls=%async_computation.7 | async-start | bytes 2359296 | tf_op jit(solution)/shard_map/all_gather | solution.py:147
  8.7 93.3 %all-gather.14.cloned.1.call-start = ((), (), s32[]{:S(2)}) async-start(), calls=%async_computation.9 | async-start | bytes 2359296 | tf_op jit(solution)/shard_map/all_gather | solution.py:146
  9.4 214.8 %all-gather.16.cloned.1.call-start = ((), (), s32[]{:S(2)}) async-start(), calls=%async_computation.10 | async-start | bytes 2359296 | tf_op jit(solution)/shard_map/all_gather | solution.py:149
  10.0 286.5 %all-reduce.8.cloned.1.call-start = ((), (), s32[]{:S(2)}) async-start(), calls=%async_computation.11 | async-start | bytes 4194304 | tf_op jit(solution)/shard_map/psum | solution.py:71
  117.5 26.1 %collective-permute-start = (bf16[512,512]{0,1:T(8,128)(2,1)}, bf16[512,512]{0,1:T(8,128)(2,1)}, u32[]{:S(2)}, u32[]{:S(2)}) collective-permute-start(bf16[512,512]{0,1:T(8,128)(2,1)} %get-tuple-element.432), channel_id=1, source_target_pairs={{0,4},{4,8},{8,12},{12,0},{1,5},{5,9},{9,13},{13,1},{2,6},{6,10},{... | collective-permute-start | bytes 1572872 | tf_op jit(solution)/shard_map/while/body/eval_jaxpr/ppermute | solution.py:16
  119.0 24.3 %collective-permute-start.3 = (s32[512]{0:T(512)S(1)}, s32[512]{0:T(512)S(1)}, u32[]{:S(2)}, u32[]{:S(2)}) collective-permute-start(s32[512]{0:T(512)S(1)} %get-tuple-element.435), channel_id=1, source_target_pairs={{0,4},{4,8},{8,12},{12,0},{1,5},{5,9},{9,13},{13,1},{2,6},{6,10},{... | collective-permute-start | bytes 6152 | tf_op jit(solution)/shard_map/while/body/eval_jaxpr/ppermute | solution.py:16
  120.5 33.8 %collective-permute-start.1 = (bf16[512,512]{0,1:T(8,128)(2,1)}, bf16[512,512]{0,1:T(8,128)(2,1)S(1)}, u32[]{:S(2)}, u32[]{:S(2)}) collective-permute-start(bf16[512,512]{0,1:T(8,128)(2,1)} %get-tuple-element.433), channel_id=1, source_target_pairs={{0,4},{4,8},{8,12},{12,0},{1,5},{5,9},{9,13},{13,1},{2,6},{6,10},{... | collective-permute-start | bytes 1572872 | tf_op jit(solution)/shard_map/while/body/eval_jaxpr/ppermute | solution.py:16
  161.1 25.4 %collective-permute-start.1 = (bf16[512,512]{0,1:T(8,128)(2,1)}, bf16[512,512]{0,1:T(8,128)(2,1)S(1)}, u32[]{:S(2)}, u32[]{:S(2)}) collective-permute-start(bf16[512,512]{0,1:T(8,128)(2,1)} %get-tuple-element.433), channel_id=1, source_target_pairs={{0,4},{4,8},{8,12},{12,0},{1,5},{5,9},{9,13},{13,1},{2,6},{6,10},{... | collective-permute-start | bytes 1572872 | tf_op jit(solution)/shard_map/while/body/eval_jaxpr/ppermute | solution.py:16
  192.3 25.4 %collective-permute-start.1 = (bf16[512,512]{0,1:T(8,128)(2,1)}, bf16[512,512]{0,1:T(8,128)(2,1)S(1)}, u32[]{:S(2)}, u32[]{:S(2)}) collective-permute-start(bf16[512,512]{0,1:T(8,128)(2,1)} %get-tuple-element.433), channel_id=1, source_target_pairs={{0,4},{4,8},{8,12},{12,0},{1,5},{5,9},{9,13},{13,1},{2,6},{6,10},{... | collective-permute-start | bytes 1572872 | tf_op jit(solution)/shard_map/while/body/eval_jaxpr/ppermute | solution.py:16
  228.6 151.3 %all-gather.20.cloned.1.call-start = ((), (), s32[]{:S(2)}) async-start(), calls=%async_computation.13 | async-start | bytes 9437184 | tf_op jit(solution)/shard_map/all_gather | solution.py:151
  229.2 232.9 %all-gather.18.cloned.1.call-start = ((), (), s32[]{:S(2)}) async-start(), calls=%async_computation.12 | async-start | bytes 9437184 | tf_op jit(solution)/shard_map/all_gather | solution.py:150
  230.0 314.3 %all-gather.22.cloned.1.call-start = ((), (), s32[]{:S(2)}) async-start(), calls=%async_computation.14 | async-start | bytes 9437184 | tf_op jit(solution)/shard_map/all_gather | solution.py:152
  230.7 409.5 %all-reduce.10.cloned.1.call-start = ((), (), s32[]{:S(2)}) async-start(), calls=%async_computation.15 | async-start | bytes 4194304 | tf_op jit(solution)/shard_map/psum | solution.py:75
  572.1 411.2 %reduce-scatter.14.cloned.1.call-start = ((), (), s32[]{:S(2)}) async-start(), calls=%async_computation.19 | async-start | bytes 2359296 | tf_op jit(solution)/shard_map/reduce_scatter | solution.py:305
  665.0 320.2 %reduce-scatter.12.cloned.1.call-start = ((), (), s32[]{:S(2)}) async-start(), calls=%async_computation.18 | async-start | bytes 2359296 | tf_op jit(solution)/shard_map/reduce_scatter | solution.py:302
  665.3 26.0 %collective-permute-start.4 = (bf16[512,512]{0,1:T(8,128)(2,1)}, bf16[512,512]{0,1:T(8,128)(2,1)S(1)}, u32[]{:S(2)}, u32[]{:S(2)}) collective-permute-start(bf16[512,512]{0,1:T(8,128)(2,1)} %get-tuple-element.471), channel_id=1, source_target_pairs={{0,4},{4,8},{8,12},{12,0},{1,5},{5,9},{9,13},{13,1},{2,6},{6,10},{... | collective-permute-start | bytes 1572872 | tf_op jit(solution)/shard_map/while/body/eval_jaxpr/ppermute | solution.py:16
  669.8 91.5 %collective-permute-start.9 = (bf16[512,512]{0,1:T(8,128)(2,1)}, bf16[512,512]{0,1:T(8,128)(2,1)}, u32[]{:S(2)}, u32[]{:S(2)}) collective-permute-start(bf16[512,512]{0,1:T(8,128)(2,1)} %get-tuple-element.477), channel_id=1, source_target_pairs={{0,4},{4,8},{8,12},{12,0},{1,5},{5,9},{9,13},{13,1},{2,6},{6,10},{... | collective-permute-start | bytes 1572872 | tf_op jit(solution)/shard_map/while/body/eval_jaxpr/ppermute | solution.py:16
  670.3 96.0 %collective-permute-start.8 = (bf16[512,512]{0,1:T(8,128)(2,1)}, bf16[512,512]{0,1:T(8,128)(2,1)}, u32[]{:S(2)}, u32[]{:S(2)}) collective-permute-start(bf16[512,512]{0,1:T(8,128)(2,1)} %get-tuple-element.476), channel_id=1, source_target_pairs={{0,4},{4,8},{8,12},{12,0},{1,5},{5,9},{9,13},{13,1},{2,6},{6,10},{... | collective-permute-start | bytes 1572872 | tf_op jit(solution)/shard_map/while/body/eval_jaxpr/ppermute | solution.py:16
  689.4 64.6 %collective-permute-start.5 = (bf16[512,512]{0,1:T(8,128)(2,1)}, bf16[512,512]{0,1:T(8,128)(2,1)S(1)}, u32[]{:S(2)}, u32[]{:S(2)}) collective-permute-start(bf16[512,512]{0,1:T(8,128)(2,1)} %get-tuple-element.472), channel_id=1, source_target_pairs={{0,4},{4,8},{8,12},{12,0},{1,5},{5,9},{9,13},{13,1},{2,6},{6,10},{... | collective-permute-start | bytes 1572872 | tf_op jit(solution)/shard_map/while/body/eval_jaxpr/ppermute | solution.py:16
  771.3 52.2 %collective-permute-start.9 = (bf16[512,512]{0,1:T(8,128)(2,1)}, bf16[512,512]{0,1:T(8,128)(2,1)}, u32[]{:S(2)}, u32[]{:S(2)}) collective-permute-start(bf16[512,512]{0,1:T(8,128)(2,1)} %get-tuple-element.477), channel_id=1, source_target_pairs={{0,4},{4,8},{8,12},{12,0},{1,5},{5,9},{9,13},{13,1},{2,6},{6,10},{... | collective-permute-start | bytes 1572872 | tf_op jit(solution)/shard_map/while/body/eval_jaxpr/ppermute | solution.py:16
  773.6 54.9 %collective-permute-start.8 = (bf16[512,512]{0,1:T(8,128)(2,1)}, bf16[512,512]{0,1:T(8,128)(2,1)}, u32[]{:S(2)}, u32[]{:S(2)}) collective-permute-start(bf16[512,512]{0,1:T(8,128)(2,1)} %get-tuple-element.476), channel_id=1, source_target_pairs={{0,4},{4,8},{8,12},{12,0},{1,5},{5,9},{9,13},{13,1},{2,6},{6,10},{... | collective-permute-start | bytes 1572872 | tf_op jit(solution)/shard_map/while/body/eval_jaxpr/ppermute | solution.py:16
  785.5 30.7 %collective-permute-start.5 = (bf16[512,512]{0,1:T(8,128)(2,1)}, bf16[512,512]{0,1:T(8,128)(2,1)S(1)}, u32[]{:S(2)}, u32[]{:S(2)}) collective-permute-start(bf16[512,512]{0,1:T(8,128)(2,1)} %get-tuple-element.472), channel_id=1, source_target_pairs={{0,4},{4,8},{8,12},{12,0},{1,5},{5,9},{9,13},{13,1},{2,6},{6,10},{... | collective-permute-start | bytes 1572872 | tf_op jit(solution)/shard_map/while/body/eval_jaxpr/ppermute | solution.py:16
  832.6 52.3 %collective-permute-start.9 = (bf16[512,512]{0,1:T(8,128)(2,1)}, bf16[512,512]{0,1:T(8,128)(2,1)}, u32[]{:S(2)}, u32[]{:S(2)}) collective-permute-start(bf16[512,512]{0,1:T(8,128)(2,1)} %get-tuple-element.477), channel_id=1, source_target_pairs={{0,4},{4,8},{8,12},{12,0},{1,5},{5,9},{9,13},{13,1},{2,6},{6,10},{... | collective-permute-start | bytes 1572872 | tf_op jit(solution)/shard_map/while/body/eval_jaxpr/ppermute | solution.py:16
  835.9 54.1 %collective-permute-start.8 = (bf16[512,512]{0,1:T(8,128)(2,1)}, bf16[512,512]{0,1:T(8,128)(2,1)}, u32[]{:S(2)}, u32[]{:S(2)}) collective-permute-start(bf16[512,512]{0,1:T(8,128)(2,1)} %get-tuple-element.476), channel_id=1, source_target_pairs={{0,4},{4,8},{8,12},{12,0},{1,5},{5,9},{9,13},{13,1},{2,6},{6,10},{... | collective-permute-start | bytes 1572872 | tf_op jit(solution)/shard_map/while/body/eval_jaxpr/ppermute | solution.py:16
  847.8 29.9 %collective-permute-start.5 = (bf16[512,512]{0,1:T(8,128)(2,1)}, bf16[512,512]{0,1:T(8,128)(2,1)S(1)}, u32[]{:S(2)}, u32[]{:S(2)}) collective-permute-start(bf16[512,512]{0,1:T(8,128)(2,1)} %get-tuple-element.472), channel_id=1, source_target_pairs={{0,4},{4,8},{8,12},{12,0},{1,5},{5,9},{9,13},{13,1},{2,6},{6,10},{... | collective-permute-start | bytes 1572872 | tf_op jit(solution)/shard_map/while/body/eval_jaxpr/ppermute | solution.py:16
  908.0 100.1 %reduce-scatter.10.cloned.1.call-start = ((), (), s32[]{:S(2)}) async-start(), calls=%async_computation.17 | async-start | bytes 2359296 | tf_op jit(solution)/shard_map/reduce_scatter | solution.py:299
  931.1 128.1 %reduce-scatter.8.cloned.1.call-start = ((), (), s32[]{:S(2)}) async-start(), calls=%async_computation.16 | async-start | bytes 2359296 | tf_op jit(solution)/shard_map/reduce_scatter | solution.py:296
  934.0 232.0 %all-reduce.12.cloned.1.call-start = ((), (), s32[]{:S(2)}) async-start(), calls=%async_computation.23 | async-start | bytes 8388608 | tf_op jit(solution)/shard_map/psum | solution.py:71
  950.5 385.3 %reduce-scatter.20.cloned.1.call-start = ((), (), s32[]{:S(2)}) async-start(), calls=%async_computation.22 | async-start | bytes 9437184 | tf_op jit(solution)/shard_map/reduce_scatter | solution.py:314
  960.8 544.9 %reduce-scatter.18.cloned.1.call-start = ((), (), s32[]{:S(2)}) async-start(), calls=%async_computation.21 | async-start | bytes 9437184 | tf_op jit(solution)/shard_map/reduce_scatter | solution.py:311
  971.0 704.8 %reduce-scatter.16.cloned.1.call-start = ((), (), s32[]{:S(2)}) async-start(), calls=%async_computation.20 | async-start | bytes 9437184 | tf_op jit(solution)/shard_map/reduce_scatter | solution.py:308
  (83 other events, 3145.1 us)
Sparse Core Ops, SparseCore 0:
  9.6 32.0 all-gather.11
  43.2 28.5 all-gather.9
  73.4 28.5 all-gather.13
  103.4 36.3 all-gather.15
  228.8 67.6 all-reduce.7
  297.9 82.0 all-gather.19
  381.5 80.5 all-gather.17
  463.7 80.5 all-gather.21
  572.2 67.9 all-reduce.9
  665.1 88.9 reduce-scatter.13
  908.1 51.4 reduce-scatter.11
  961.8 46.2 reduce-scatter.9
  1011.0 48.2 reduce-scatter.7
  1063.2 102.8 all-reduce.11
  1168.2 167.5 reduce-scatter.19
  1337.9 167.8 reduce-scatter.17
  1507.9 167.8 reduce-scatter.15
where the time goes:
time: 1690 us
  waiting for transfers between devices  1300 us (77%)
  matrix products  186 us (11%)
  other arithmetic  64.5 us (4%)
  blocking collectives  50.7 us (3%)
  starting transfers between devices  34.9 us (2%)
  local copies, waits for them, and re-layouts  32.6 us (2%)
    ppermute x32, waiting for transfers between devices, passed_along(): return lax.ppermute(value, axis, pairs)  252 us
    reduce_scatter x1, waiting for transfers between devices, on_device(): lax.psum_scatter(grad_wup.astype(jnp.bfloat16), ('shard', 'context'), sca...  167 us
    reduce_scatter x1, waiting for transfers between devices, on_device(): lax.psum_scatter(grad_wgate.astype(jnp.bfloat16), ('shard', 'context'), s...  167 us
    psum x2, waiting for transfers between devices, branch_total(): lax.psum(partial_sum.astype(jnp.bfloat16), 'tensor').astype(jnp.float32)  158 us
    reduce_scatter x1, waiting for transfers between devices, on_device(): lax.psum_scatter(grad_wdown.astype(jnp.bfloat16), ('shard', 'context'), s...  138 us
    all_gather x1, waiting for transfers between devices, on_device(): lax.all_gather(w_up, ('shard', 'context'), axis=0, tiled=True)  78.6 us
    all_gather x1, waiting for transfers between devices, on_device(): lax.all_gather(w_gate, ('shard', 'context'), axis=0, tiled=True)  71.6 us
    all_gather x1, waiting for transfers between devices, on_device(): lax.all_gather(w_down, ('shard', 'context'), axis=0, tiled=True)  71.6 us
  transfers between devices with their start and end apart: 49, of which 28 were waited for; matrix products, arithmetic and copies ran while one was open for 13% of the time, Pallas kernels for 0%

commit v1 on v0

--- a/solution.py
+++ b/solution.py
@@ -72,7 +72,9 @@
 
 
 def input_total(partial_sum):
-    return lax.psum(partial_sum.astype(jnp.bfloat16), "tensor").astype(jnp.float32)
+    return jnp.sum(lax.all_gather(partial_sum.astype(jnp.bfloat16), axis_name="tensor"), 0).astype(
+        jnp.float32
+    )
 
 
 def pass_grads(grad_key, grad_value):

time: 1690 us -> 1730 us (1.024)
  starting transfers between devices: 34.9 us -> 140 us
  waiting for transfers between devices: 1300 us -> 1210 us
    all_gather x0 -> x2, waiting for transfers between devices: none -> 173 us  [input_total(): lax.all_gather(partial_sum.astype(jnp.bfloat16), axis_name='tensor')]
    reduce_scatter x1, waiting for transfers between devices: 167 us -> 0.01 us  [on_device(): lax.psum_scatter(grad_wup.astype(jnp.bfloat16), ('shard', 'context'), sca...]
    reduce_scatter x1, waiting for transfers between devices: 138 us -> 0.01 us  [on_device(): lax.psum_scatter(grad_wdown.astype(jnp.bfloat16), ('shard', 'context'), s...]
    ppermute x32, starting transfers between devices: 33 us -> 139 us  [passed_along(): return lax.ppermute(value, axis, pairs)]
    ppermute x32, waiting for transfers between devices: 252 us -> 356 us  [passed_along(): return lax.ppermute(value, axis, pairs)]
    psum x1 -> x0, waiting for transfers between devices: 67.9 us -> none  [input_total(): lax.psum(partial_sum.astype(jnp.bfloat16), 'tensor').astype(jnp.float32)]
    psum x2, waiting for transfers between devices: 158 us -> 97.2 us  [branch_total(): lax.psum(partial_sum.astype(jnp.bfloat16), 'tensor').astype(jnp.float32)]
    reduce_scatter x1, waiting for transfers between devices: 0.01 us -> 49.7 us  [on_device(): lax.psum_scatter(grad_wv.astype(jnp.bfloat16), ('shard', 'context'), scat...]
  transfers between devices with their start and end apart: 49 -> 50, of which waited for: 28 -> 28; matrix products, arithmetic and copies ran while one was open for 13% -> 14% of each run, Pallas kernels for 0% -> 0%
where the time goes in v1:
time: 1730 us; the launch traced here: 1720 us
  waiting for transfers between devices  1210 us (70%)
  matrix products  203 us (12%)
  starting transfers between devices  140 us (8%)
  other arithmetic  79.8 us (5%)
  blocking collectives  47.3 us (3%)
  local copies, waits for them, and re-layouts  31 us (2%)
    ppermute x32, waiting for transfers between devices, passed_along(): return lax.ppermute(value, axis, pairs)  356 us
    all_gather x2, waiting for transfers between devices, input_total(): lax.all_gather(partial_sum.astype(jnp.bfloat16), axis_name='tensor')  173 us
    reduce_scatter x1, waiting for transfers between devices, on_device(): lax.psum_scatter(grad_wgate.astype(jnp.bfloat16), ('shard', 'context'), s...  151 us
    ppermute x32, starting transfers between devices, passed_along(): return lax.ppermute(value, axis, pairs)  139 us
    psum x2, waiting for transfers between devices, branch_total(): lax.psum(partial_sum.astype(jnp.bfloat16), 'tensor').astype(jnp.float32)  97.2 us
    all_gather x1, waiting for transfers between devices, on_device(): lax.all_gather(w_up, ('shard', 'context'), axis=0, tiled=True)  78.6 us
    all_gather x1, waiting for transfers between devices, on_device(): lax.all_gather(w_gate, ('shard', 'context'), axis=0, tiled=True)  71.6 us
    all_gather x1, waiting for transfers between devices, on_device(): lax.all_gather(w_down, ('shard', 'context'), axis=0, tiled=True)  71.6 us
  transfers between devices with their start and end apart: 50, of which 28 were waited for; matrix products, arithmetic and copies ran while one was open for 14% of the time, Pallas kernels for 0%

profile of v1, /device:TPU:0, one launch (start us, length us, event | category | flops | bytes accessed | tf_op | source)
XLA Modules:
  0.0 1723.1 jit_solution(11396122312231476411)
XLA Ops:
  15.9 18.3 %all-gather.2 = bf16[8,1,256]{2,1,0:T(2,128)(2,1)S(1)} all-gather(bf16[1,1,256]{2,1,0:T(2,128)(2,1)S(1)} %reshape.453), channel_id=1, replica_groups=mesh['shard'=2,'context'=4,'tensor'=4] {'shard','context'}, dimensions={0}, use_global_device_ids=true | all-gather | bytes 4608 | tf_op jit(solution)/shard_map/all_gather | solution.py:155
  46.8 25.0 %all-gather.14.cloned.1.call-done = bf16[2048,512]{1,0:T(8,128)(2,1)} async-done(((bf16[256,512]{1,0:T(8,128)(2,1)}), bf16[2048,512]{1,0:T(8,128)(2,1)}) %all-gather.14.cloned.1.call-update) | async-done | bytes 2097168 | tf_op jit(solution)/shard_map/all_gather | solution.py:149
  79.9 22.1 %all-gather.18.cloned.1.call-done = bf16[2048,512]{1,0:T(8,128)(2,1)} async-done(((bf16[256,512]{1,0:T(8,128)(2,1)}), bf16[2048,512]{1,0:T(8,128)(2,1)}) %all-gather.18.cloned.1.call-update) | async-done | bytes 2097168 | tf_op jit(solution)/shard_map/all_gather | solution.py:148
  117.3 105.5 %while.44 = (s32[]{:T(128)}, bf16[512,512]{0,1:T(8,128)(2,1)}, bf16[512,512]{0,1:T(8,128)(2,1)}, s32[512]{0:T(512)S(1)}, s32[512]{0:T(512)S(1)}, /*index=5*/f32[...) while((s32[]{:T(128)}, bf16[512,512]{0,1:T(8,128)(2,1)}, ...), condition=%wide.region_6.7_spmd, body=%wide.region_3.6_spmd.sunk | while | flops 565452800 | bytes 44859724 | solution.py:194
  122.5 20.8 %collective-permute-done.3 = s32[512]{0:T(512)S(1)} collective-permute-done((s32[512]{0:T(512)S(1)}, s32[512]{0:T(512)S(1)}, u32[]{:S(2)}, u32[]{:S(2)}) %collective-permute-start.3) | collective-permute-done | bytes 2080 | tf_op jit(solution)/shard_map/while/body/eval_jaxpr/ppermute | solution.py:16
  230.6 12.8 all-gather.3
  243.4 52.8 %all-reduce.6.cloned.1.call-done = bf16[512,2048]{1,0:T(8,128)(2,1)} async-done(((bf16[512,2048]{1,0:T(8,128)(2,1)}), bf16[512,2048]{1,0:T(8,128)(2,1)}) %all-reduce.6.cloned.1.call-update) | async-done | bytes 2097168 | tf_op jit(solution)/shard_map/psum | solution.py:71
  301.1 78.6 %all-gather.24.cloned.1.call-done = bf16[2048,2048]{1,0:T(8,128)(2,1)} async-done(((bf16[256,2048]{1,0:T(8,128)(2,1)}), bf16[2048,2048]{1,0:T(8,128)(2,1)}) %all-gather.24.cloned.1.call-update) | async-done | bytes 8388624 | tf_op jit(solution)/shard_map/all_gather | solution.py:153
  390.3 71.6 %all-gather.22.cloned.1.call-done = bf16[2048,2048]{1,0:T(8,128)(2,1)} async-done(((bf16[256,2048]{1,0:T(8,128)(2,1)}), bf16[2048,2048]{1,0:T(8,128)(2,1)}) %all-gather.22.cloned.1.call-update) | async-done | bytes 8388624 | tf_op jit(solution)/shard_map/all_gather | solution.py:152
  472.5 71.6 %all-gather.26.cloned.1.call-done = bf16[2048,2048]{1,0:T(8,128)(2,1)} async-done(((bf16[256,2048]{1,0:T(8,128)(2,1)}), bf16[2048,2048]{1,0:T(8,128)(2,1)}) %all-gather.26.cloned.1.call-update) | async-done | bytes 8388624 | tf_op jit(solution)/shard_map/all_gather | solution.py:154
  544.1 26.0 %multiply_convert_fusion.2 = (bf16[512,2048]{1,0:T(8,128)(2,1)S(1)}, bf16[512,2048]{1,0:T(8,128)(2,1)S(1)}, bf16[512,2048]{1,0:T(8,128)(2,1)}) fusion(f32[512,2048]{1,0:T(8,128)} %fusion.90, f32[512,2048]{1,0:T(8,128)} %fusion.91, bf16[2048,2048]{1,0:T(8,128)(2,1)} %all-gather.26.cloned.1.call-done, bf16[1,512,2048]{2,1,0:T(8,128)(2,1)} %param.29), kind=kOutput, calls=%fused_computation.68 | convolution fusion | flops 4310695936 | bytes 25165824 | tf_op jit(solution)/shard_map/dot_general | solution.py:227
  583.9 86.1 %all-gather.28.cloned.1.call-done = bf16[2048,2048]{1,0:T(8,128)(2,1)} async-done(((bf16[512,2048]{1,0:T(8,128)(2,1)}), bf16[2048,2048]{1,0:T(8,128)(2,1)}) %all-gather.28.cloned.1.call-update) | async-done | bytes 8388624 | tf_op jit(solution)/shard_map/all_gather | solution.py:75
  736.3 370.6 %while.45 = (s32[]{:T(128)}, bf16[512,512]{0,1:T(8,128)(2,1)}, bf16[512,512]{0,1:T(8,128)(2,1)}, s32[512]{0:T(512)S(1)}, s32[512]{0:T(512)S(1)}, /*index=5*/f32[...) while((s32[]{:T(128)}, bf16[512,512]{0,1:T(8,128)(2,1)}, ...), condition=%wide.region_14.15_spmd, body=%wide.region_13.14_spmd.sunk | while | flops 1372061696 | bytes 71647696 | solution.py:267
  742.7 17.3 %collective-permute-done.7 = s32[512]{0:T(512)S(1)} collective-permute-done((s32[512]{0:T(512)S(1)}, s32[512]{0:T(512)S(1)}, u32[]{:S(2)}, u32[]{:S(2)}) %collective-permute-start.7) | collective-permute-done | bytes 2080 | tf_op jit(solution)/shard_map/while/body/eval_jaxpr/ppermute | solution.py:16
  764.7 61.5 %collective-permute-done.5 = bf16[512,512]{0,1:T(8,128)(2,1)S(1)} collective-permute-done((bf16[512,512]{0,1:T(8,128)(2,1)}, bf16[512,512]{0,1:T(8,128)(2,1)S(1)}, u32[]{:S(2)}, u32[]{:S(2)}) %collective-permute-start.5) | collective-permute-done | bytes 524320 | tf_op jit(solution)/shard_map/while/body/eval_jaxpr/ppermute | solution.py:16
  840.9 27.5 %collective-permute-start.4 = (bf16[512,512]{0,1:T(8,128)(2,1)}, bf16[512,512]{0,1:T(8,128)(2,1)S(1)}, u32[]{:S(2)}, u32[]{:S(2)}) collective-permute-start(bf16[512,512]{0,1:T(8,128)(2,1)} %get-tuple-element.469), channel_id=1, source_target_pairs={{0,4},{4,8},{8,12},{12,0},{1,5},{5,9},{9,13},{13,1},{2,6},{6,10},{... | collective-permute-start | bytes 1572872 | tf_op jit(solution)/shard_map/while/body/eval_jaxpr/ppermute | solution.py:16
  873.3 23.0 %collective-permute-done.7 = s32[512]{0:T(512)S(1)} collective-permute-done((s32[512]{0:T(512)S(1)}, s32[512]{0:T(512)S(1)}, u32[]{:S(2)}, u32[]{:S(2)}) %collective-permute-start.7) | collective-permute-done | bytes 2080 | tf_op jit(solution)/shard_map/while/body/eval_jaxpr/ppermute | solution.py:16
  902.6 58.8 %collective-permute-done.5 = bf16[512,512]{0,1:T(8,128)(2,1)S(1)} collective-permute-done((bf16[512,512]{0,1:T(8,128)(2,1)}, bf16[512,512]{0,1:T(8,128)(2,1)S(1)}, u32[]{:S(2)}, u32[]{:S(2)}) %collective-permute-start.5) | collective-permute-done | bytes 524320 | tf_op jit(solution)/shard_map/while/body/eval_jaxpr/ppermute | solution.py:16
  976.1 22.5 %collective-permute-start.4 = (bf16[512,512]{0,1:T(8,128)(2,1)}, bf16[512,512]{0,1:T(8,128)(2,1)S(1)}, u32[]{:S(2)}, u32[]{:S(2)}) collective-permute-start(bf16[512,512]{0,1:T(8,128)(2,1)} %get-tuple-element.469), channel_id=1, source_target_pairs={{0,4},{4,8},{8,12},{12,0},{1,5},{5,9},{9,13},{13,1},{2,6},{6,10},{... | collective-permute-start | bytes 1572872 | tf_op jit(solution)/shard_map/while/body/eval_jaxpr/ppermute | solution.py:16
  1003.6 22.2 %collective-permute-done.7 = s32[512]{0:T(512)S(1)} collective-permute-done((s32[512]{0:T(512)S(1)}, s32[512]{0:T(512)S(1)}, u32[]{:S(2)}, u32[]{:S(2)}) %collective-permute-start.7) | collective-permute-done | bytes 2080 | tf_op jit(solution)/shard_map/while/body/eval_jaxpr/ppermute | solution.py:16
  1034.6 57.7 %collective-permute-done.5 = bf16[512,512]{0,1:T(8,128)(2,1)S(1)} collective-permute-done((bf16[512,512]{0,1:T(8,128)(2,1)}, bf16[512,512]{0,1:T(8,128)(2,1)S(1)}, u32[]{:S(2)}, u32[]{:S(2)}) %collective-permute-start.5) | collective-permute-done | bytes 524320 | tf_op jit(solution)/shard_map/while/body/eval_jaxpr/ppermute | solution.py:16
  1107.0 29.3 %collective-permute-start.11 = (bf16[512,512]{0,1:T(8,128)(2,1)}, bf16[512,512]{0,1:T(8,128)(2,1)S(1)}, u32[]{:S(2)}, u32[]{:S(2)}) collective-permute-start(bf16[512,512]{0,1:T(8,128)(2,1)} %get-tuple-element.149), channel_id=1, source_target_pairs={{0,4},{4,8},{8,12},{12,0},{1,5},{5,9},{9,13},{13,1},{2,6},{6,10},{... | collective-permute-start | bytes 1572872 | tf_op jit(solution)/shard_map/ppermute | solution.py:16
  1136.3 26.6 %collective-permute-done.11 = bf16[512,512]{0,1:T(8,128)(2,1)S(1)} collective-permute-done((bf16[512,512]{0,1:T(8,128)(2,1)}, bf16[512,512]{0,1:T(8,128)(2,1)S(1)}, u32[]{:S(2)}, u32[]{:S(2)}) %collective-permute-start.11) | collective-permute-done | bytes 524320 | tf_op jit(solution)/shard_map/ppermute | solution.py:16
  1166.6 13.0 collective-permute-start.10
  1179.6 28.2 %collective-permute-done.10 = bf16[512,512]{0,1:T(8,128)(2,1)S(1)} collective-permute-done((bf16[512,512]{0,1:T(8,128)(2,1)S(1)}, bf16[512,512]{0,1:T(8,128)(2,1)S(1)}, u32[]{:S(2)}, u32[]{:S(2)}) %collective-permute-start.10) | collective-permute-done | bytes 524320 | tf_op jit(solution)/shard_map/ppermute | solution.py:16
  1241.6 151.4 %reduce-scatter.16.cloned.1.call-done = bf16[256,2048]{1,0:T(8,128)(2,1)} async-done(((bf16[2048,2048]{1,0:T(8,128)(2,1)}), bf16[256,2048]{1,0:T(8,128)(2,1)}) %reduce-scatter.16.cloned.1.call-update) | async-done | bytes 1048592 | tf_op jit(solution)/shard_map/reduce_scatter | solution.py:310
  1395.8 49.7 %reduce-scatter.12.cloned.1.call-done = bf16[256,512]{1,0:T(8,128)(2,1)} async-done(((bf16[2048,512]{1,0:T(8,128)(2,1)}), bf16[256,512]{1,0:T(8,128)(2,1)}) %reduce-scatter.12.cloned.1.call-update) | async-done | bytes 262160 | tf_op jit(solution)/shard_map/reduce_scatter | solution.py:304
  1447.3 48.6 %reduce-scatter.10.cloned.1.call-done = bf16[256,512]{1,0:T(8,128)(2,1)} async-done(((bf16[2048,512]{1,0:T(8,128)(2,1)}), bf16[256,512]{1,0:T(8,128)(2,1)}) %reduce-scatter.10.cloned.1.call-update) | async-done | bytes 262160 | tf_op jit(solution)/shard_map/reduce_scatter | solution.py:301
  1497.7 48.6 %reduce-scatter.8.cloned.1.call-done = bf16[256,512]{1,0:T(8,128)(2,1)} async-done(((bf16[2048,512]{1,0:T(8,128)(2,1)}), bf16[256,512]{1,0:T(8,128)(2,1)}) %reduce-scatter.8.cloned.1.call-update) | async-done | bytes 262160 | tf_op jit(solution)/shard_map/reduce_scatter | solution.py:298
  1548.2 87.1 %all-gather.30.cloned.1.call-done = bf16[2048,2048]{1,0:T(8,128)(2,1)} async-done(((bf16[512,2048]{1,0:T(8,128)(2,1)}), bf16[2048,2048]{1,0:T(8,128)(2,1)}) %all-gather.30.cloned.1.call-update) | async-done | bytes 8388624 | tf_op jit(solution)/shard_map/all_gather | solution.py:75
  1645.9 16.2 all-reduce.2
  1663.4 44.4 %all-reduce.8.cloned.1.call-done = bf16[512,2048]{1,0:T(8,128)(2,1)} async-done(((bf16[512,2048]{1,0:T(8,128)(2,1)}), bf16[512,2048]{1,0:T(8,128)(2,1)}) %all-reduce.8.cloned.1.call-update) | async-done | bytes 2097168 | tf_op jit(solution)/shard_map/psum | solution.py:71
  (358 shorter events, 387.0 us)
Async XLA Ops:
  7.2 34.5 %all-gather.16.cloned.1.call-start = ((), (), s32[]{:S(2)}) async-start(), calls=%async_computation.8 | async-start | bytes 2359296 | tf_op jit(solution)/shard_map/all_gather | solution.py:150
  7.9 63.9 %all-gather.14.cloned.1.call-start = ((), (), s32[]{:S(2)}) async-start(), calls=%async_computation.7 | async-start | bytes 2359296 | tf_op jit(solution)/shard_map/all_gather | solution.py:149
  8.7 93.3 %all-gather.18.cloned.1.call-start = ((), (), s32[]{:S(2)}) async-start(), calls=%async_computation.9 | async-start | bytes 2359296 | tf_op jit(solution)/shard_map/all_gather | solution.py:148
  9.4 214.8 %all-gather.20.cloned.1.call-start = ((), (), s32[]{:S(2)}) async-start(), calls=%async_computation.10 | async-start | bytes 2359296 | tf_op jit(solution)/shard_map/all_gather | solution.py:151
  10.0 286.3 %all-reduce.6.cloned.1.call-start = ((), (), s32[]{:S(2)}) async-start(), calls=%async_computation.11 | async-start | bytes 4194304 | tf_op jit(solution)/shard_map/psum | solution.py:71
  120.5 33.8 %collective-permute-start.1 = (bf16[512,512]{0,1:T(8,128)(2,1)}, bf16[512,512]{0,1:T(8,128)(2,1)S(1)}, u32[]{:S(2)}, u32[]{:S(2)}) collective-permute-start(bf16[512,512]{0,1:T(8,128)(2,1)} %get-tuple-element.431), channel_id=1, source_target_pairs={{0,4},{4,8},{8,12},{12,0},{1,5},{5,9},{9,13},{13,1},{2,6},{6,10},{... | collective-permute-start | bytes 1572872 | tf_op jit(solution)/shard_map/while/body/eval_jaxpr/ppermute | solution.py:16
  228.5 151.3 %all-gather.24.cloned.1.call-start = ((), (), s32[]{:S(2)}) async-start(), calls=%async_computation.13 | async-start | bytes 9437184 | tf_op jit(solution)/shard_map/all_gather | solution.py:153
  229.0 232.9 %all-gather.22.cloned.1.call-start = ((), (), s32[]{:S(2)}) async-start(), calls=%async_computation.12 | async-start | bytes 9437184 | tf_op jit(solution)/shard_map/all_gather | solution.py:152
  229.8 314.3 %all-gather.26.cloned.1.call-start = ((), (), s32[]{:S(2)}) async-start(), calls=%async_computation.14 | async-start | bytes 9437184 | tf_op jit(solution)/shard_map/all_gather | solution.py:154
  230.5 439.4 %all-gather.28.cloned.1.call-start = ((), (), s32[]{:S(2)}) async-start(), calls=%async_computation.23 | async-start | bytes 10485760 | tf_op jit(solution)/shard_map/all_gather | solution.py:75
  583.8 650.6 %reduce-scatter.14.cloned.1.call-start = ((), (), s32[]{:S(2)}) async-start(), calls=%async_computation.19 | async-start | bytes 2359296 | tf_op jit(solution)/shard_map/reduce_scatter | solution.py:307
  685.8 550.4 %reduce-scatter.20.cloned.1.call-start = ((), (), s32[]{:S(2)}) async-start(), calls=%async_computation.22 | async-start | bytes 9437184 | tf_op jit(solution)/shard_map/reduce_scatter | solution.py:316
  696.0 542.8 %reduce-scatter.18.cloned.1.call-start = ((), (), s32[]{:S(2)}) async-start(), calls=%async_computation.21 | async-start | bytes 9437184 | tf_op jit(solution)/shard_map/reduce_scatter | solution.py:313
  706.6 686.4 %reduce-scatter.16.cloned.1.call-start = ((), (), s32[]{:S(2)}) async-start(), calls=%async_computation.20 | async-start | bytes 9437184 | tf_op jit(solution)/shard_map/reduce_scatter | solution.py:310
  716.7 728.8 %reduce-scatter.12.cloned.1.call-start = ((), (), s32[]{:S(2)}) async-start(), calls=%async_computation.18 | async-start | bytes 2359296 | tf_op jit(solution)/shard_map/reduce_scatter | solution.py:304
  740.8 92.7 %collective-permute-start.9 = (bf16[512,512]{0,1:T(8,128)(2,1)}, bf16[512,512]{0,1:T(8,128)(2,1)}, u32[]{:S(2)}, u32[]{:S(2)}) collective-permute-start(bf16[512,512]{0,1:T(8,128)(2,1)} %get-tuple-element.475), channel_id=1, source_target_pairs={{0,4},{4,8},{8,12},{12,0},{1,5},{5,9},{9,13},{13,1},{2,6},{6,10},{... | collective-permute-start | bytes 1572872 | tf_op jit(solution)/shard_map/while/body/eval_jaxpr/ppermute | solution.py:16
  741.3 97.2 %collective-permute-start.8 = (bf16[512,512]{0,1:T(8,128)(2,1)}, bf16[512,512]{0,1:T(8,128)(2,1)}, u32[]{:S(2)}, u32[]{:S(2)}) collective-permute-start(bf16[512,512]{0,1:T(8,128)(2,1)} %get-tuple-element.474), channel_id=1, source_target_pairs={{0,4},{4,8},{8,12},{12,0},{1,5},{5,9},{9,13},{13,1},{2,6},{6,10},{... | collective-permute-start | bytes 1572872 | tf_op jit(solution)/shard_map/while/body/eval_jaxpr/ppermute | solution.py:16
  760.1 66.2 %collective-permute-start.5 = (bf16[512,512]{0,1:T(8,128)(2,1)}, bf16[512,512]{0,1:T(8,128)(2,1)S(1)}, u32[]{:S(2)}, u32[]{:S(2)}) collective-permute-start(bf16[512,512]{0,1:T(8,128)(2,1)} %get-tuple-element.470), channel_id=1, source_target_pairs={{0,4},{4,8},{8,12},{12,0},{1,5},{5,9},{9,13},{13,1},{2,6},{6,10},{... | collective-permute-start | bytes 1572872 | tf_op jit(solution)/shard_map/while/body/eval_jaxpr/ppermute | solution.py:16
  840.9 60.4 %collective-permute-start.4 = (bf16[512,512]{0,1:T(8,128)(2,1)}, bf16[512,512]{0,1:T(8,128)(2,1)S(1)}, u32[]{:S(2)}, u32[]{:S(2)}) collective-permute-start(bf16[512,512]{0,1:T(8,128)(2,1)} %get-tuple-element.469), channel_id=1, source_target_pairs={{0,4},{4,8},{8,12},{12,0},{1,5},{5,9},{9,13},{13,1},{2,6},{6,10},{... | collective-permute-start | bytes 1572872 | tf_op jit(solution)/shard_map/while/body/eval_jaxpr/ppermute | solution.py:16
  873.1 95.6 %collective-permute-start.9 = (bf16[512,512]{0,1:T(8,128)(2,1)}, bf16[512,512]{0,1:T(8,128)(2,1)}, u32[]{:S(2)}, u32[]{:S(2)}) collective-permute-start(bf16[512,512]{0,1:T(8,128)(2,1)} %get-tuple-element.475), channel_id=1, source_target_pairs={{0,4},{4,8},{8,12},{12,0},{1,5},{5,9},{9,13},{13,1},{2,6},{6,10},{... | collective-permute-start | bytes 1572872 | tf_op jit(solution)/shard_map/while/body/eval_jaxpr/ppermute | solution.py:16
  873.1 100.6 %collective-permute-start.8 = (bf16[512,512]{0,1:T(8,128)(2,1)}, bf16[512,512]{0,1:T(8,128)(2,1)}, u32[]{:S(2)}, u32[]{:S(2)}) collective-permute-start(bf16[512,512]{0,1:T(8,128)(2,1)} %get-tuple-element.474), channel_id=1, source_target_pairs={{0,4},{4,8},{8,12},{12,0},{1,5},{5,9},{9,13},{13,1},{2,6},{6,10},{... | collective-permute-start | bytes 1572872 | tf_op jit(solution)/shard_map/while/body/eval_jaxpr/ppermute | solution.py:16
  896.3 65.2 %collective-permute-start.5 = (bf16[512,512]{0,1:T(8,128)(2,1)}, bf16[512,512]{0,1:T(8,128)(2,1)S(1)}, u32[]{:S(2)}, u32[]{:S(2)}) collective-permute-start(bf16[512,512]{0,1:T(8,128)(2,1)} %get-tuple-element.470), channel_id=1, source_target_pairs={{0,4},{4,8},{8,12},{12,0},{1,5},{5,9},{9,13},{13,1},{2,6},{6,10},{... | collective-permute-start | bytes 1572872 | tf_op jit(solution)/shard_map/while/body/eval_jaxpr/ppermute | solution.py:16
  976.1 57.2 %collective-permute-start.4 = (bf16[512,512]{0,1:T(8,128)(2,1)}, bf16[512,512]{0,1:T(8,128)(2,1)S(1)}, u32[]{:S(2)}, u32[]{:S(2)}) collective-permute-start(bf16[512,512]{0,1:T(8,128)(2,1)} %get-tuple-element.469), channel_id=1, source_target_pairs={{0,4},{4,8},{8,12},{12,0},{1,5},{5,9},{9,13},{13,1},{2,6},{6,10},{... | collective-permute-start | bytes 1572872 | tf_op jit(solution)/shard_map/while/body/eval_jaxpr/ppermute | solution.py:16
  1002.6 97.0 %collective-permute-start.9 = (bf16[512,512]{0,1:T(8,128)(2,1)}, bf16[512,512]{0,1:T(8,128)(2,1)}, u32[]{:S(2)}, u32[]{:S(2)}) collective-permute-start(bf16[512,512]{0,1:T(8,128)(2,1)} %get-tuple-element.475), channel_id=1, source_target_pairs={{0,4},{4,8},{8,12},{12,0},{1,5},{5,9},{9,13},{13,1},{2,6},{6,10},{... | collective-permute-start | bytes 1572872 | tf_op jit(solution)/shard_map/while/body/eval_jaxpr/ppermute | solution.py:16
  1002.6 102.0 %collective-permute-start.8 = (bf16[512,512]{0,1:T(8,128)(2,1)}, bf16[512,512]{0,1:T(8,128)(2,1)}, u32[]{:S(2)}, u32[]{:S(2)}) collective-permute-start(bf16[512,512]{0,1:T(8,128)(2,1)} %get-tuple-element.474), channel_id=1, source_target_pairs={{0,4},{4,8},{8,12},{12,0},{1,5},{5,9},{9,13},{13,1},{2,6},{6,10},{... | collective-permute-start | bytes 1572872 | tf_op jit(solution)/shard_map/while/body/eval_jaxpr/ppermute | solution.py:16
  1025.7 66.6 %collective-permute-start.5 = (bf16[512,512]{0,1:T(8,128)(2,1)}, bf16[512,512]{0,1:T(8,128)(2,1)S(1)}, u32[]{:S(2)}, u32[]{:S(2)}) collective-permute-start(bf16[512,512]{0,1:T(8,128)(2,1)} %get-tuple-element.470), channel_id=1, source_target_pairs={{0,4},{4,8},{8,12},{12,0},{1,5},{5,9},{9,13},{13,1},{2,6},{6,10},{... | collective-permute-start | bytes 1572872 | tf_op jit(solution)/shard_map/while/body/eval_jaxpr/ppermute | solution.py:16
  1107.0 56.0 %collective-permute-start.11 = (bf16[512,512]{0,1:T(8,128)(2,1)}, bf16[512,512]{0,1:T(8,128)(2,1)S(1)}, u32[]{:S(2)}, u32[]{:S(2)}) collective-permute-start(bf16[512,512]{0,1:T(8,128)(2,1)} %get-tuple-element.149), channel_id=1, source_target_pairs={{0,4},{4,8},{8,12},{12,0},{1,5},{5,9},{9,13},{13,1},{2,6},{6,10},{... | collective-permute-start | bytes 1572872 | tf_op jit(solution)/shard_map/ppermute | solution.py:16
  1166.6 329.4 %reduce-scatter.10.cloned.1.call-start = ((), (), s32[]{:S(2)}) async-start(), calls=%async_computation.17 | async-start | bytes 2359296 | tf_op jit(solution)/shard_map/reduce_scatter | solution.py:301
  1166.6 41.2 %collective-permute-start.10 = (bf16[512,512]{0,1:T(8,128)(2,1)S(1)}, bf16[512,512]{0,1:T(8,128)(2,1)S(1)}, u32[]{:S(2)}, u32[]{:S(2)}) collective-permute-start(bf16[512,512]{0,1:T(8,128)(2,1)S(1)} %copy-done.30), channel_id=1, source_target_pairs={{0,4},{4,8},{8,12},{12,0},{1,5},{5,9},{9,13},{13,1},{2,6},{6,10},{... | collective-permute-start | bytes 1572872 | tf_op jit(solution)/shard_map/ppermute | solution.py:16
  1212.4 334.0 %reduce-scatter.8.cloned.1.call-start = ((), (), s32[]{:S(2)}) async-start(), calls=%async_computation.16 | async-start | bytes 2359296 | tf_op jit(solution)/shard_map/reduce_scatter | solution.py:298
  1215.3 420.0 %all-gather.30.cloned.1.call-start = ((), (), s32[]{:S(2)}) async-start(), calls=%async_computation.24 | async-start | bytes 10485760 | tf_op jit(solution)/shard_map/all_gather | solution.py:75
  1222.8 484.9 %all-reduce.8.cloned.1.call-start = ((), (), s32[]{:S(2)}) async-start(), calls=%async_computation.15 | async-start | bytes 4194304 | tf_op jit(solution)/shard_map/psum | solution.py:71
  (78 other events, 2425.5 us)
Sparse Core Ops, SparseCore 0:
  9.6 32.0 all-gather.15
  43.2 28.5 all-gather.13
  73.4 28.5 all-gather.17
  103.4 36.2 all-gather.19
  228.6 67.6 all-reduce.5
  297.7 82.0 all-gather.23
  381.4 80.5 all-gather.21
  463.5 80.5 all-gather.25
  584.0 85.9 all-gather.27
  685.9 49.0 reduce-scatter.13
  737.3 251.9 reduce-scatter.19
  991.5 232.7 reduce-scatter.17
  1226.6 166.3 reduce-scatter.15
  1395.1 50.2 reduce-scatter.11
  1447.6 48.2 reduce-scatter.9
  1498.1 48.2 reduce-scatter.7
  1548.6 86.6 all-gather.29
  1638.3 69.4 all-reduce.7
